TPU v7x, 32 devices: a whole 2x2x4 slice. The times are simulated.
32 devices in a mesh: groups: 2 (over x), blk: 16 (over z, y, core).
Axes of the slice: x: 2, y: 2, z: 4, core: 2. Of those that a mesh axis runs over, the one named last changes fastest.
Arguments:
- paths: bfloat16 [4096, 512], P(('groups', 'blk')), parts along dimension 0, may hold values from -6 to 6
- deltas: bfloat16 [4096, 512], P(('groups', 'blk')), parts along dimension 0, may hold values from -6 to 6
- payoffs: bfloat16 [4096], P(('groups', 'blk')), parts along dimension 0, may hold values from -6 to 6
- counts: int32 [32, 16], P('groups'), parts along dimension 0, may hold values from 0 to 8, as said below
- w_first: bfloat16 [1024, 1024], P(('groups', 'blk')), parts along dimension 0, may hold values from -0.25 to 0.25
- w_second: bfloat16 [2048, 1024], P(('groups', 'blk')), parts along dimension 0, may hold values from -0.1875 to 0.1875
- w_out: bfloat16 [2048], P('groups'), parts along dimension 0, may hold values from -0.1875 to 0.1875
- mom_first: float32 [1024, 1024], P(('groups', 'blk')), parts along dimension 0, may hold values from -6 to 6
- mom_second: float32 [2048, 1024], P(('groups', 'blk')), parts along dimension 0, may hold values from -6 to 6
- mom_out: float32 [2048], P('groups'), parts along dimension 0, may hold values from -6 to 6
Outputs:
- new_first: float32 [1024, 1024], P(('groups', 'blk')), parts along dimension 0
- new_second: float32 [2048, 1024], P(('groups', 'blk')), parts along dimension 0
- new_out: float32 [2048], P('groups'), parts along dimension 0
There are 2 independent parts, one for each index of `groups`. A program takes and returns all parts, laid end to end along the dimension named above; each array names one. Nothing has to cross between parts.
Inputs may be any that keep to these rules, and one draw needn't show every extreme that they name: Source s hands its valid paths, slot 0 onward, to the trainers in order: counts[s, d] of them to trainer d. Every trainer receives 64 paths or fewer in all, and one receives exactly 64; one source hands 8 to every trainer.
All inputs are finite; a program needn't handle non-finite values.
Results may differ from a plain program's by a relative error of at most 0.00035.
The roundings to bfloat16 on the way count: a program that leaves them out, or rounds other values in their place, can miss the bound.
Values may be sent and summed in bfloat16 or wider, within the bound.
No kernel may reach another device: no remote copies, remote signals or barrier semaphores. Data moves between devices by JAX's collectives and lax.ppermute only.
A program may use at most 64 MiB of HBM per device.

v0:
```python
import jax
import jax.numpy as jnp
from jax import lax
from jax.sharding import PartitionSpec as P


def rows_product(left, right):
    return lax.dot_general(
        left, right, (((0,), (0,)), ((), ())), preferred_element_type=jnp.float32
    )


def twin_terms(x_rows, z_rows, y_rows, mask, w_one, w_two, w_three):
    w_outf = w_three.astype(jnp.float32)
    a_one = jnp.dot(x_rows, w_one, preferred_element_type=jnp.float32)
    s_one = jax.nn.sigmoid(a_one)
    h_one = jax.nn.softplus(a_one).astype(jnp.bfloat16)
    a_two = jnp.dot(h_one, w_two, preferred_element_type=jnp.float32)
    s_two = jax.nn.sigmoid(a_two)
    h_two = jax.nn.softplus(a_two)
    value = jnp.sum(h_two * w_outf[None, :], axis=1)
    g_two = (s_two * w_outf[None, :]).astype(jnp.bfloat16)
    c_one = lax.dot_general(
        g_two, w_two, (((1,), (1,)), ((), ())), preferred_element_type=jnp.float32
    )
    g_one = (c_one * s_one).astype(jnp.bfloat16)
    slope = lax.dot_general(
        g_one, w_one, (((1,), (1,)), ((), ())), preferred_element_type=jnp.float32
    )
    e_value = 2.0 * mask * (value - y_rows.astype(jnp.float32))
    e_slope = (2.0 * mask[:, None] * (slope - z_rows.astype(jnp.float32))).astype(jnp.bfloat16)
    e_gone = jnp.dot(e_slope, w_one, preferred_element_type=jnp.float32)
    e_cone = (e_gone * s_one).astype(jnp.bfloat16)
    e_sone = e_gone * c_one
    e_gtwo = jnp.dot(e_cone, w_two, preferred_element_type=jnp.float32)
    grad_three = jnp.sum(e_gtwo * s_two + e_value[:, None] * h_two, axis=0)
    e_atwo = (
        e_gtwo * w_outf[None, :] * s_two * (1.0 - s_two)
        + e_value[:, None] * w_outf[None, :] * s_two
    ).astype(jnp.bfloat16)
    e_hone = lax.dot_general(
        e_atwo, w_two, (((1,), (1,)), ((), ())), preferred_element_type=jnp.float32
    )
    e_aone = (e_sone * s_one * (1.0 - s_one) + e_hone * s_one).astype(jnp.bfloat16)
    return (e_slope, g_one, e_aone, e_cone, g_two, h_one, e_atwo, grad_three)


def normalized(grad):
    return grad / jnp.sqrt(jnp.mean(grad * grad, axis=-1, keepdims=True) + 1e-06)


def per_device(
    paths, deltas, payoffs, counts, w_first, w_second, w_out, mom_first, mom_second, mom_out
):
    position = lax.axis_index("blk")
    rows_dev = paths.shape[0]
    w_one, w_two = (
        lax.all_gather(w_first, "blk", axis=0, tiled=True),
        lax.all_gather(w_second, "blk", axis=0, tiled=True),
    )
    sending = lax.dynamic_index_in_dim(counts, position, 0, keepdims=False)
    x_rows, z_rows, y_rows = (paths, deltas, payoffs)
    total = jnp.sum(sending)
    mask = (jnp.arange(rows_dev, dtype=jnp.int32) < total).astype(jnp.float32)
    e_slope, g_one, e_aone, e_cone, g_two, h_one, e_atwo, grad_three = twin_terms(
        x_rows, z_rows, y_rows, mask, w_one, w_two, w_out
    )
    grad_one = lax.psum_scatter(
        rows_product(x_rows, e_aone) + rows_product(e_slope, g_one),
        "blk",
        scatter_dimension=0,
        tiled=True,
    )
    grad_two = lax.psum_scatter(
        rows_product(e_cone, g_two) + rows_product(h_one, e_atwo),
        "blk",
        scatter_dimension=0,
        tiled=True,
    )
    grad_out = lax.psum(grad_three, "blk")
    new_first = 0.8 * mom_first + 0.2 * normalized(grad_one)
    new_second = 0.8 * mom_second + 0.2 * normalized(grad_two)
    new_out = 0.8 * mom_out + 0.2 * normalized(grad_out)
    return (new_first, new_second, new_out)


def solution(mesh):
    in_specs = (
        P(("groups", "blk"), None),
        P(("groups", "blk"), None),
        P(("groups", "blk")),
        P("groups", None),
        P(("groups", "blk"), None),
        P(("groups", "blk"), None),
        P("groups"),
        P(("groups", "blk"), None),
        P(("groups", "blk"), None),
        P("groups"),
    )
    out_specs = (P(("groups", "blk"), None), P(("groups", "blk"), None), P("groups"))
    return jax.shard_map(
        per_device, mesh=mesh, in_specs=in_specs, out_specs=out_specs, check_vma=False
    )
```

profile of v0, /device:TPU:0, one launch (start us, length us, event | category | flops | bytes accessed | tf_op | source)
XLA Modules:
  0.0 254.4 jit_solution(2150444523015975469)
XLA Ops:
  7.2 0.0 copy-start
  7.2 0.0 all-gather.3.cloned.1.call-start
  7.2 0.7 all-gather.3.cloned.1.call-update
  7.9 0.0 all-gather.5.cloned.1.call-start
  8.0 0.7 all-gather.5.cloned.1.call-update
  8.7 0.0 reduce-scatter.7.cloned.1.call-start
  8.7 0.7 convert_element_type.33
  9.4 1.3 dynamic-slice_reduce_fusion
  10.7 0.6 compare_select_fusion.2
  11.4 39.5 %all-gather.3.cloned.1.call-done = bf16[512,1024]{1,0:T(8,128)(2,1)} async-done(((bf16[32,1024]{1,0:T(8,128)(2,1)}), bf16[512,1024]{1,0:T(8,128)(2,1)}) %all-gather.3.cloned.1.call-update) | async-done | bytes 1048592 | tf_op jit(solution)/shard_map/all_gather | solution.py:58
  50.8 0.0 copy-done
  50.9 1.5 fusion.17
  52.4 0.0 copy-start.11
  52.4 41.0 %all-gather.5.cloned.1.call-done = bf16[1024,1024]{1,0:T(8,128)(2,1)} async-done(((bf16[64,1024]{1,0:T(8,128)(2,1)}), bf16[1024,1024]{1,0:T(8,128)(2,1)}) %all-gather.5.cloned.1.call-update) | async-done | bytes 2097168 | tf_op jit(solution)/shard_map/all_gather | solution.py:59
  93.4 2.6 %multiply_reduce_fusion.1 = (f32[128]{0:T(128)S(1)}, f32[128,1024]{1,0:T(8,128)S(1)}) fusion(f32[1024]{0:T(1024)S(1)} %convert_element_type.33, bf16[1024,1024]{1,0:T(8,128)(2,1)} %all-gather.5.cloned.1.call-done, f32[128,1024]{1,0:T(8,128)S(1)} %fusion.17), kind=kOutput, calls=%fused_computation.16 | convolution fusion | flops 270401408 | bytes 3150336 | tf_op jit(solution)/shard_map/dot_general | solution.py:18
  96.0 0.0 copy-done.11
  96.0 0.7 subtract_multiply_fusion
  96.7 0.0 copy-done.2
  96.7 0.0 copy-start.8
  96.7 1.7 multiply_convert_fusion.1
  98.4 0.0 copy-done.1
  98.4 0.5 fusion.4
  98.9 1.1 multiply_convert_fusion
  100.0 0.0 copy-done.3
  100.0 0.9 add_reduce_fusion
  100.9 3.0 %fusion.2 = f32[1024,512]{1,0:T(8,128)S(1)} fusion(bf16[128,512]{1,0:T(8,128)(2,1)S(1)} %copy-done, bf16[128,1024]{1,0:T(8,128)(2,1)S(1)} %get-tuple-element.10, bf16[1024,1024]{1,0:T(8,128)(2,1)} %all-gather.5.cloned.1.call-done, f32[128,1024]{1,0:T(8,128)} %get-tuple-element.14, f32[128,1024]{1,0:T(8,128)} %get-tuple-element.12, f32[128,1024]{1,0:T(8,128)S(1)} %fusion.17), kind=kOutput, calls=%fused_computation.7 | convolution fusion | flops 403963904 | bytes 6160384 | tf_op jit(solution)/shard_map/dot_general | solution.py:8
  103.9 1.8 bitcast_add_fusion
  105.7 2.9 %copy.20 = f32[512,1024]{1,0:T(8,128)} copy(f32[512,1024]{0,1:T(8,128)} %bitcast_add_fusion) | data formatting | bytes 4194304
  108.6 0.0 reduce-scatter.7.cloned.1.call-update
  108.7 0.0 reduce-scatter.5.cloned.1.call-start
  108.7 1.0 copy-done.4
  109.7 0.1 copy-done.6
  109.7 0.8 fusion.11
  110.5 2.8 %convolution_add_fusion = f32[1024,1024]{1,0:T(8,128)} fusion(f32[1024,1024]{1,0:T(8,128)S(1)} %fusion.11, bf16[128,1024]{1,0:T(8,128)(2,1)S(1)} %get-tuple-element.10, f32[128,1024]{1,0:T(8,128)S(1)} %fusion.17), kind=kOutput, calls=%fused_computation | convolution fusion | flops 270401536 | bytes 9175040 | tf_op jit(solution)/shard_map/dot_general | solution.py:8
  113.3 0.0 reduce-scatter.5.cloned.1.call-update
  113.3 0.9 copy-done.9
  114.2 0.2 copy.16
  114.4 31.6 %psum.7 = f32[1024]{0:T(1024)S(1)} all-reduce(f32[1024]{0:T(1024)S(1)} %get-tuple-element.9), channel_id=1, replica_groups=mesh['groups'=2,'blk'=16] {'blk'}, use_global_device_ids=true, to_apply=%region_7.8 | all-reduce | flops 1024 | bytes 8192 | tf_op jit(solution)/shard_map/psum | solution.py:80
  146.1 0.6 multiply_reduce_fusion.3
  147.4 0.6 multiply_add_fusion.2
  148.0 21.5 %reduce-scatter.7.cloned.1.call-done = f32[32,1024]{1,0:T(8,128)} async-done(((f32[512,1024]{1,0:T(8,128)}), f32[32,1024]{1,0:T(8,128)}) %reduce-scatter.7.cloned.1.call-update) | async-done | bytes 131088
  169.5 1.1 copy.21
  170.6 0.2 multiply_reduce_fusion
  170.8 0.1 multiply_add_fusion
  170.9 0.8 copy.18
  171.7 73.3 %reduce-scatter.5.cloned.1.call-done = f32[64,1024]{1,0:T(8,128)} async-done(((f32[1024,1024]{1,0:T(8,128)}), f32[64,1024]{1,0:T(8,128)}) %reduce-scatter.5.cloned.1.call-update) | async-done | bytes 262160 | tf_op jit(solution)/shard_map/reduce_scatter | solution.py:74
  245.0 1.1 multiply_reduce_fusion.2
  246.1 1.8 multiply_add_fusion.1
  (15 shorter events, 0.0 us)
Async XLA Ops:
  7.2 43.7 %copy-start = (bf16[128,512]{1,0:T(8,128)(2,1)S(1)}, bf16[128,512]{1,0:T(8,128)(2,1)}, u32[]{:S(2)}) copy-start(bf16[128,512]{1,0:T(8,128)(2,1)} %param.10) | copy-start | bytes 393220
  7.2 43.7 %all-gather.3.cloned.1.call-start = ((), (), s32[]{:S(2)}) async-start(), calls=%async_computation.2 | async-start | bytes 1114112 | tf_op jit(solution)/shard_map/all_gather | solution.py:58
  7.9 85.4 %all-gather.5.cloned.1.call-start = ((), (), s32[]{:S(2)}) async-start(), calls=%async_computation.3 | async-start | bytes 2228224 | tf_op jit(solution)/shard_map/all_gather | solution.py:59
  8.7 160.8 %reduce-scatter.7.cloned.1.call-start = ((), (), s32[]{:S(2)}) async-start(), calls=%async_computation.5 | async-start | bytes 2228224
  52.4 43.6 %copy-start.11 = (bf16[128]{0:T(256)(128)(2,1)S(1)}, bf16[128]{0:T(256)(128)(2,1)}, u32[]{:S(2)}) copy-start(bf16[128]{0:T(256)(128)(2,1)} %param.12) | copy-start | bytes 772
  93.4 3.3 %copy-start.2 = (bf16[1024,1024]{1,0:T(8,128)(2,1)S(1)}, bf16[1024,1024]{1,0:T(8,128)(2,1)}, u32[]{:S(2)}) copy-start(bf16[1024,1024]{1,0:T(8,128)(2,1)} %all-gather.5.cloned.1.call-done) | copy-start | bytes 6291460
  96.0 4.0 %copy-start.3 = (f32[128,1024]{1,0:T(8,128)}, f32[128,1024]{1,0:T(8,128)S(1)}, u32[]{:S(2)}) copy-start(f32[128,1024]{1,0:T(8,128)S(1)} %get-tuple-element.16) | copy-start | bytes 1572868
  96.7 1.7 copy-start.1
  96.7 1.7 copy-start.8
  100.0 0.9 copy-start.5
  108.6 1.0 copy-start.4
  108.6 1.1 copy-start.6
  108.7 136.4 %reduce-scatter.5.cloned.1.call-start = ((), (), s32[]{:S(2)}) async-start(), calls=%async_computation.4 | async-start | bytes 4456448 | tf_op jit(solution)/shard_map/reduce_scatter | solution.py:74
  113.3 0.9 copy-start.9
  113.3 34.0 %copy-start.10 = (f32[1024]{0:T(1024)S(1)}, f32[1024]{0:T(1024)}, u32[]{:S(2)}) copy-start(f32[1024]{0:T(1024)} %param.19) | copy-start | bytes 12292
  114.2 131.9 %copy-start.7 = (f32[64,1024]{1,0:T(8,128)S(1)}, f32[64,1024]{1,0:T(8,128)}, u32[]{:S(2)}) copy-start(f32[64,1024]{1,0:T(8,128)} %param.18) | copy-start | bytes 786436
Sparse Core Ops, SparseCore 0:
  10.2 40.6 all-gather.2
  53.0 40.3 all-gather.4
  108.8 60.6 reduce-scatter.6
  173.7 71.2 reduce-scatter.4
where the time goes:
time: 255 us; the launch traced here: 254 us
  waiting for transfers between devices  177 us (69%)
  blocking collectives  31.6 us (12%)
  matrix products  16.7 us (7%)
  between operations  14.6 us (6%)
  other arithmetic  7.63 us (3%)
  local copies, waits for them, and re-layouts  6.99 us (3%)
    reduce_scatter x1, waiting for transfers between devices, per_device(): lax.psum_scatter(rows_product(e_cone, g_two) + rows_product(h_one, e_atwo...  73.3 us
    all_gather x1, waiting for transfers between devices, per_device(): lax.all_gather(w_second, 'blk', axis=0, tiled=True)  41 us
    all_gather x1, waiting for transfers between devices, per_device(): lax.all_gather(w_first, 'blk', axis=0, tiled=True)  39.5 us
    psum x1, blocking collectives, per_device(): grad_out = lax.psum(grad_three, 'blk')  31.6 us
    unnamed x5, waiting for transfers between devices  22.9 us
    dot_general x4, matrix products, rows_product(): lax.dot_general(left, right, (((0,), (0,)), ((), ())), preferred_element_...  8.39 us
    unnamed x28, local copies, waits for them, and re-layouts  6.99 us
  transfers between devices with their start and end apart: 4, of which 4 were waited for; matrix products, arithmetic and copies ran while one was open for 4% of the time, Pallas kernels for 0%

commit v1 on v0

--- a/solution.py
+++ b/solution.py
@@ -1,7 +1,39 @@
+import functools
 import jax
 import jax.numpy as jnp
 from jax import lax
 from jax.sharding import PartitionSpec as P
+
+
+def obtain_lots_all(here_x, ndim_at):
+    y = list(here_x.shape[1:])
+    y[ndim_at] *= here_x.shape[0]
+    heard = jnp.moveaxis(here_x, 0, ndim_at).reshape(y)
+    return heard
+
+
+def _make_knots(z_in, net_axis, along_dim):
+    world_n = lax.psum(1, net_axis)
+    shaped = range(world_n)
+    opened = map(lambda k: (k, (k + 1) % world_n), shaped)
+    buffers = list(opened)
+    stack_in = [(p, q) for q, p in buffers]
+    h_now, inter = ([], [])
+    for jj in range(world_n - 1):
+        if jj % 2 == 0:
+            h_now.append(lax.ppermute(h_now[-1] if h_now else z_in, net_axis, buffers))
+        else:
+            inter.append(lax.ppermute(inter[-1] if inter else z_in, net_axis, stack_in))
+    part_now = jnp.stack([*h_now[::-1], z_in, *inter], 0)
+    known = len(h_now)
+    piece_next = lax.axis_index(net_axis)
+    carry = piece_next - known
+    part_now = part_now[(jnp.arange(world_n) - carry) % world_n]
+    v_now = obtain_lots_all(part_now, along_dim)
+    return v_now
+
+
+form_spans_now = functools.partial(_make_knots, net_axis="blk", along_dim=0)
 
 
 def rows_product(left, right):
@@ -54,10 +86,7 @@
 ):
     position = lax.axis_index("blk")
     rows_dev = paths.shape[0]
-    w_one, w_two = (
-        lax.all_gather(w_first, "blk", axis=0, tiled=True),
-        lax.all_gather(w_second, "blk", axis=0, tiled=True),
-    )
+    w_one, w_two = (form_spans_now(w_first), lax.all_gather(w_second, "blk", axis=0, tiled=True))
     sending = lax.dynamic_index_in_dim(counts, position, 0, keepdims=False)
     x_rows, z_rows, y_rows = (paths, deltas, payoffs)
     total = jnp.sum(sending)

time: 255 us -> 241 us (0.945)
  waiting for transfers between devices: 177 us -> 129 us
  starting transfers between devices: 0.16 us -> 31.8 us
    all_gather x1 -> x0, waiting for transfers between devices: 39.5 us -> none  [per_device(): lax.all_gather(w_first, 'blk', axis=0, tiled=True)]
    ppermute x0 -> x15, starting transfers between devices: none -> 31.7 us  [the longest x7 31.2 us: _make_knots(): inter.append(lax.ppermute(inter[-1] if inter else z_in, net_axis, stack_in))]
    all_gather x1, waiting for transfers between devices: 41 us -> 13.5 us  [per_device(): lax.all_gather(w_second, 'blk', axis=0, tiled=True)]
    ppermute x0 -> x15, waiting for transfers between devices: none -> 20.3 us  [the longest x8 15.8 us: _make_knots(): h_now.append(lax.ppermute(h_now[-1] if h_now else z_in, net_axis, buffers))]
    unnamed x5 -> x4, waiting for transfers between devices: 22.9 us -> 21.2 us
    unnamed x28 -> x41, local copies, waits for them, and re-layouts: 6.99 us -> 7.91 us
  transfers between devices with their start and end apart: 4 -> 18, of which waited for: 4 -> 16; matrix products, arithmetic and copies ran while one was open for 4% -> 5% of each run, Pallas kernels for 0% -> 0%
where the time goes in v1:
time: 241 us; the launch traced here: 240 us
  waiting for transfers between devices  129 us (54%)
  blocking collectives  32.2 us (13%)
  starting transfers between devices  31.8 us (13%)
  matrix products  16.7 us (7%)
  between operations  14.7 us (6%)
  local copies, waits for them, and re-layouts  8.53 us (4%)
  other arithmetic  7.63 us (3%)
    reduce_scatter x1, waiting for transfers between devices, per_device(): lax.psum_scatter(rows_product(e_cone, g_two) + rows_product(h_one, e_atwo...  73.6 us
    psum x1, blocking collectives, per_device(): grad_out = lax.psum(grad_three, 'blk')  32.2 us
    ppermute x7, starting transfers between devices, _make_knots(): inter.append(lax.ppermute(inter[-1] if inter else z_in, net_axis, stack_in))  31.2 us
    unnamed x4, waiting for transfers between devices  21.2 us
    ppermute x8, waiting for transfers between devices, _make_knots(): h_now.append(lax.ppermute(h_now[-1] if h_now else z_in, net_axis, buffers))  15.8 us
    all_gather x1, waiting for transfers between devices, per_device(): lax.all_gather(w_second, 'blk', axis=0, tiled=True)  13.5 us
    dot_general x4, matrix products, rows_product(): lax.dot_general(left, right, (((0,), (0,)), ((), ())), preferred_element_...  8.48 us
    unnamed x41, local copies, waits for them, and re-layouts  7.91 us
  transfers between devices with their start and end apart: 18, of which 16 were waited for; matrix products, arithmetic and copies ran while one was open for 5% of the time, Pallas kernels for 0%

profile of v1, /device:TPU:0, one launch (start us, length us, event | category | flops | bytes accessed | tf_op | source)
XLA Modules:
  0.0 240.2 jit_solution(3157014332496207057)
XLA Ops:
  7.2 0.5 collective-permute-start
  7.7 7.2 %collective-permute-done = bf16[32,1024]{1,0:T(8,128)(2,1)S(1)} collective-permute-done((bf16[32,1024]{1,0:T(8,128)(2,1)}, bf16[32,1024]{1,0:T(8,128)(2,1)S(1)}, u32[]{:S(2)}, u32[]{:S(2)}) %collective-permute-start) | collective-permute-done | bytes 65568 | tf_op jit(solution)/shard_map/ppermute | solution.py:24
  14.9 4.4 %collective-permute-start.8 = (bf16[32,1024]{1,0:T(8,128)(2,1)}, bf16[32,1024]{1,0:T(8,128)(2,1)S(1)}, u32[]{:S(2)}, u32[]{:S(2)}) collective-permute-start(bf16[32,1024]{1,0:T(8,128)(2,1)} %param.14), channel_id=1, source_target_pairs={{1,0},{2,1},{3,2},{4,3},{5,4},{6,5},{7,6},{8,7},{9,8},{10,9},{11,1... | collective-permute-start | bytes 196616 | tf_op jit(solution)/shard_map/ppermute | solution.py:26
  19.3 1.9 collective-permute-done.1
  21.6 4.4 %collective-permute-start.9 = (bf16[32,1024]{1,0:T(8,128)(2,1)S(1)}, bf16[32,1024]{1,0:T(8,128)(2,1)S(1)}, u32[]{:S(2)}, u32[]{:S(2)}) collective-permute-start(bf16[32,1024]{1,0:T(8,128)(2,1)S(1)} %collective-permute-done.8), channel_id=1, source_target_pairs={{1,0},{2,1},{3,2},{4,3},{5,4},{6,5},{7,6},{8,7},{9,8},{10,9},{11,1... | collective-permute-start | bytes 196616 | tf_op jit(solution)/shard_map/ppermute | solution.py:26
  25.9 1.7 collective-permute-done.2
  27.8 4.5 %collective-permute-start.10 = (bf16[32,1024]{1,0:T(8,128)(2,1)S(1)}, bf16[32,1024]{1,0:T(8,128)(2,1)S(1)}, u32[]{:S(2)}, u32[]{:S(2)}) collective-permute-start(bf16[32,1024]{1,0:T(8,128)(2,1)S(1)} %collective-permute-done.9), channel_id=1, source_target_pairs={{1,0},{2,1},{3,2},{4,3},{5,4},{6,5},{7,6},{8,7},{9,8},{10,9},{11,1... | collective-permute-start | bytes 196616 | tf_op jit(solution)/shard_map/ppermute | solution.py:26
  32.3 1.8 collective-permute-done.3
  34.2 1.3 dynamic-slice_reduce_fusion
  35.5 4.4 %collective-permute-start.11 = (bf16[32,1024]{1,0:T(8,128)(2,1)S(1)}, bf16[32,1024]{1,0:T(8,128)(2,1)S(1)}, u32[]{:S(2)}, u32[]{:S(2)}) collective-permute-start(bf16[32,1024]{1,0:T(8,128)(2,1)S(1)} %collective-permute-done.10), channel_id=1, source_target_pairs={{1,0},{2,1},{3,2},{4,3},{5,4},{6,5},{7,6},{8,7},{9,8},{10,9},{11,1... | collective-permute-start | bytes 196616 | tf_op jit(solution)/shard_map/ppermute | solution.py:26
  40.0 0.6 collective-permute-done.4
  40.5 1.3 collective-permute-done.11
  41.9 4.5 %collective-permute-start.12 = (bf16[32,1024]{1,0:T(8,128)(2,1)S(1)}, bf16[32,1024]{1,0:T(8,128)(2,1)S(1)}, u32[]{:S(2)}, u32[]{:S(2)}) collective-permute-start(bf16[32,1024]{1,0:T(8,128)(2,1)S(1)} %collective-permute-done.11), channel_id=1, source_target_pairs={{1,0},{2,1},{3,2},{4,3},{5,4},{6,5},{7,6},{8,7},{9,8},{10,9},{11,1... | collective-permute-start | bytes 196616 | tf_op jit(solution)/shard_map/ppermute | solution.py:26
  46.3 0.6 collective-permute-done.5
  47.0 1.3 collective-permute-done.12
  48.3 4.5 %collective-permute-start.13 = (bf16[32,1024]{1,0:T(8,128)(2,1)S(1)}, bf16[32,1024]{1,0:T(8,128)(2,1)S(1)}, u32[]{:S(2)}, u32[]{:S(2)}) collective-permute-start(bf16[32,1024]{1,0:T(8,128)(2,1)S(1)} %collective-permute-done.12), channel_id=1, source_target_pairs={{1,0},{2,1},{3,2},{4,3},{5,4},{6,5},{7,6},{8,7},{9,8},{10,9},{11,1... | collective-permute-start | bytes 196616 | tf_op jit(solution)/shard_map/ppermute | solution.py:26
  52.8 1.4 collective-permute-done.6
  54.2 0.6 compare_select_fusion.5
  54.8 0.7 convert_element_type.33
  55.5 4.4 %collective-permute-start.14 = (bf16[32,1024]{1,0:T(8,128)(2,1)S(1)}, bf16[32,1024]{1,0:T(8,128)(2,1)S(1)}, u32[]{:S(2)}, u32[]{:S(2)}) collective-permute-start(bf16[32,1024]{1,0:T(8,128)(2,1)S(1)} %collective-permute-done.13), channel_id=1, source_target_pairs={{1,0},{2,1},{3,2},{4,3},{5,4},{6,5},{7,6},{8,7},{9,8},{10,9},{11,1... | collective-permute-start | bytes 196616 | tf_op jit(solution)/shard_map/ppermute | solution.py:26
  60.0 0.6 collective-permute-done.7
  60.7 0.9 bitcast_dynamic-update-slice_fusion.7
  61.6 1.5 collective-permute-done.14
  63.1 0.6 gather_fusion
  63.7 0.5 convolution_bitcast_fusion
  64.2 13.5 %all-gather.2.cloned.1.call-done = bf16[1024,1024]{1,0:T(8,128)(2,1)} async-done(((bf16[64,1024]{1,0:T(8,128)(2,1)}), bf16[1024,1024]{1,0:T(8,128)(2,1)}) %all-gather.2.cloned.1.call-update) | async-done | bytes 2097168 | tf_op jit(solution)/shard_map/all_gather | solution.py:89
  77.7 2.9 %multiply_reduce_fusion.1 = (f32[128]{0:T(128)S(1)}, f32[128,1024]{0,1:T(8,128)S(1)}) fusion(f32[1024]{0:T(1024)S(1)} %convert_element_type.33, bf16[1024,1024]{1,0:T(8,128)(2,1)} %all-gather.2.cloned.1.call-done, f32[128,1024]{0,1:T(8,128)S(1)} %convolution_bitcast_fusion), kind=kOutput, calls=%fused_computation.18 | convolution fusion | flops 270401408 | bytes 3150336 | tf_op jit(solution)/shard_map/dot_general | solution.py:50
  80.7 1.6 multiply_convert_fusion.1
  82.3 0.5 fusion.4
  82.8 1.4 multiply_convert_fusion
  84.2 0.6 subtract_multiply_fusion
  84.8 1.4 add_reduce_fusion
  86.2 3.2 %fusion.2 = f32[1024,512]{1,0:T(8,128)S(1)} fusion(bf16[128,512]{1,0:T(8,128)(2,1)S(1)} %copy-done, bf16[1024,1024]{1,0:T(8,128)(2,1)} %all-gather.2.cloned.1.call-done, bf16[128,1024]{0,1:T(8,128)(2,1)S(1)} %get-tuple-element.10, f32[128,1024]{0,1:T(8,128)} %get-tuple-element.14, f32[128,1024]{0,1:T(8,128)} %get-tuple-element.12, ...), kind=kOutput, calls=%fused_computation.9 | convolution fusion | flops 403963904 | bytes 6160384 | tf_op jit(solution)/shard_map/dot_general | solution.py:40
  89.4 1.7 bitcast_add_fusion
  91.1 2.9 %copy.48 = f32[512,1024]{1,0:T(8,128)} copy(f32[512,1024]{0,1:T(8,128)} %bitcast_add_fusion) | data formatting | bytes 4194304
  94.1 1.0 copy-done.3
  95.1 0.8 fusion.17
  96.0 2.7 %convolution_add_fusion = f32[1024,1024]{1,0:T(8,128)} fusion(f32[1024,1024]{1,0:T(8,128)S(1)} %fusion.17, bf16[128,1024]{0,1:T(8,128)(2,1)S(1)} %get-tuple-element.10, f32[128,1024]{0,1:T(8,128)S(1)} %convolution_bitcast_fusion), kind=kOutput, calls=%fused_computation.1 | convolution fusion | flops 270401536 | bytes 9175040 | tf_op jit(solution)/shard_map/dot_general | solution.py:40
  98.7 0.9 copy-done.8
  99.8 32.2 %psum.7 = f32[1024]{0:T(1024)S(1)} all-reduce(f32[1024]{0:T(1024)S(1)} %get-tuple-element.9), channel_id=1, replica_groups=mesh['groups'=2,'blk'=16] {'blk'}, use_global_device_ids=true, to_apply=%region_7.8 | all-reduce | flops 1024 | bytes 8192 | tf_op jit(solution)/shard_map/psum | solution.py:109
  132.0 0.6 multiply_reduce_fusion.3
  133.3 0.6 multiply_add_fusion.2
  133.9 21.1 %reduce-scatter.7.cloned.1.call-done = f32[32,1024]{1,0:T(8,128)} async-done(((f32[512,1024]{1,0:T(8,128)}), f32[32,1024]{1,0:T(8,128)}) %reduce-scatter.7.cloned.1.call-update) | async-done | bytes 131088
  155.0 1.1 copy.49
  156.4 0.8 copy.42
  157.2 73.6 %reduce-scatter.5.cloned.1.call-done = f32[64,1024]{1,0:T(8,128)} async-done(((f32[1024,1024]{1,0:T(8,128)}), f32[64,1024]{1,0:T(8,128)}) %reduce-scatter.5.cloned.1.call-update) | async-done | bytes 262160 | tf_op jit(solution)/shard_map/reduce_scatter | solution.py:103
  230.8 1.1 multiply_reduce_fusion.2
  231.9 1.8 multiply_add_fusion.1
  (59 shorter events, 1.3 us)
Async XLA Ops:
  7.2 56.6 %copy-start = (bf16[128,512]{1,0:T(8,128)(2,1)S(1)}, bf16[128,512]{1,0:T(8,128)(2,1)}, u32[]{:S(2)}) copy-start(bf16[128,512]{1,0:T(8,128)(2,1)} %param.10) | copy-start | bytes 393220
  7.2 70.5 %all-gather.2.cloned.1.call-start = ((), (), s32[]{:S(2)}) async-start(), calls=%async_computation.2 | async-start | bytes 2228224 | tf_op jit(solution)/shard_map/all_gather | solution.py:89
  7.2 7.7 %collective-permute-start = (bf16[32,1024]{1,0:T(8,128)(2,1)}, bf16[32,1024]{1,0:T(8,128)(2,1)S(1)}, u32[]{:S(2)}, u32[]{:S(2)}) collective-permute-start(bf16[32,1024]{1,0:T(8,128)(2,1)} %param.14), channel_id=1, source_target_pairs={{0,1},{1,2},{2,3},{3,4},{4,5},{5,6},{6,7},{7,8},{8,9},{9,10},{10,1... | collective-permute-start | bytes 196616 | tf_op jit(solution)/shard_map/ppermute | solution.py:24
  14.9 6.4 %collective-permute-start.1 = (bf16[32,1024]{1,0:T(8,128)(2,1)S(1)}, bf16[32,1024]{1,0:T(8,128)(2,1)S(1)}, u32[]{:S(2)}, u32[]{:S(2)}) collective-permute-start(bf16[32,1024]{1,0:T(8,128)(2,1)S(1)} %collective-permute-done), channel_id=1, source_target_pairs={{0,1},{1,2},{2,3},{3,4},{4,5},{5,6},{6,7},{7,8},{8,9},{9,10},{10,1... | collective-permute-start | bytes 196616 | tf_op jit(solution)/shard_map/ppermute | solution.py:24
  14.9 6.7 %collective-permute-start.8 = (bf16[32,1024]{1,0:T(8,128)(2,1)}, bf16[32,1024]{1,0:T(8,128)(2,1)S(1)}, u32[]{:S(2)}, u32[]{:S(2)}) collective-permute-start(bf16[32,1024]{1,0:T(8,128)(2,1)} %param.14), channel_id=1, source_target_pairs={{1,0},{2,1},{3,2},{4,3},{5,4},{6,5},{7,6},{8,7},{9,8},{10,9},{11,1... | collective-permute-start | bytes 196616 | tf_op jit(solution)/shard_map/ppermute | solution.py:26
  21.3 6.4 %collective-permute-start.2 = (bf16[32,1024]{1,0:T(8,128)(2,1)S(1)}, bf16[32,1024]{1,0:T(8,128)(2,1)S(1)}, u32[]{:S(2)}, u32[]{:S(2)}) collective-permute-start(bf16[32,1024]{1,0:T(8,128)(2,1)S(1)} %collective-permute-done.1), channel_id=1, source_target_pairs={{0,1},{1,2},{2,3},{3,4},{4,5},{5,6},{6,7},{7,8},{8,9},{9,10},{10,1... | collective-permute-start | bytes 196616 | tf_op jit(solution)/shard_map/ppermute | solution.py:24
  21.6 6.3 %collective-permute-start.9 = (bf16[32,1024]{1,0:T(8,128)(2,1)S(1)}, bf16[32,1024]{1,0:T(8,128)(2,1)S(1)}, u32[]{:S(2)}, u32[]{:S(2)}) collective-permute-start(bf16[32,1024]{1,0:T(8,128)(2,1)S(1)} %collective-permute-done.8), channel_id=1, source_target_pairs={{1,0},{2,1},{3,2},{4,3},{5,4},{6,5},{7,6},{8,7},{9,8},{10,9},{11,1... | collective-permute-start | bytes 196616 | tf_op jit(solution)/shard_map/ppermute | solution.py:26
  27.7 6.4 %collective-permute-start.3 = (bf16[32,1024]{1,0:T(8,128)(2,1)S(1)}, bf16[32,1024]{1,0:T(8,128)(2,1)S(1)}, u32[]{:S(2)}, u32[]{:S(2)}) collective-permute-start(bf16[32,1024]{1,0:T(8,128)(2,1)S(1)} %collective-permute-done.2), channel_id=1, source_target_pairs={{0,1},{1,2},{2,3},{3,4},{4,5},{5,6},{6,7},{7,8},{8,9},{9,10},{10,1... | collective-permute-start | bytes 196616 | tf_op jit(solution)/shard_map/ppermute | solution.py:24
  27.8 7.7 %collective-permute-start.10 = (bf16[32,1024]{1,0:T(8,128)(2,1)S(1)}, bf16[32,1024]{1,0:T(8,128)(2,1)S(1)}, u32[]{:S(2)}, u32[]{:S(2)}) collective-permute-start(bf16[32,1024]{1,0:T(8,128)(2,1)S(1)} %collective-permute-done.9), channel_id=1, source_target_pairs={{1,0},{2,1},{3,2},{4,3},{5,4},{6,5},{7,6},{8,7},{9,8},{10,9},{11,1... | collective-permute-start | bytes 196616 | tf_op jit(solution)/shard_map/ppermute | solution.py:26
  34.1 6.4 %collective-permute-start.4 = (bf16[32,1024]{1,0:T(8,128)(2,1)S(1)}, bf16[32,1024]{1,0:T(8,128)(2,1)S(1)}, u32[]{:S(2)}, u32[]{:S(2)}) collective-permute-start(bf16[32,1024]{1,0:T(8,128)(2,1)S(1)} %collective-permute-done.3), channel_id=1, source_target_pairs={{0,1},{1,2},{2,3},{3,4},{4,5},{5,6},{6,7},{7,8},{8,9},{9,10},{10,1... | collective-permute-start | bytes 196616 | tf_op jit(solution)/shard_map/ppermute | solution.py:24
  34.1 120.9 %reduce-scatter.7.cloned.1.call-start = ((), (), s32[]{:S(2)}) async-start(), calls=%async_computation.4 | async-start | bytes 2228224
  35.5 6.3 %collective-permute-start.11 = (bf16[32,1024]{1,0:T(8,128)(2,1)S(1)}, bf16[32,1024]{1,0:T(8,128)(2,1)S(1)}, u32[]{:S(2)}, u32[]{:S(2)}) collective-permute-start(bf16[32,1024]{1,0:T(8,128)(2,1)S(1)} %collective-permute-done.10), channel_id=1, source_target_pairs={{1,0},{2,1},{3,2},{4,3},{5,4},{6,5},{7,6},{8,7},{9,8},{10,9},{11,1... | collective-permute-start | bytes 196616 | tf_op jit(solution)/shard_map/ppermute | solution.py:26
  40.5 6.4 %collective-permute-start.5 = (bf16[32,1024]{1,0:T(8,128)(2,1)S(1)}, bf16[32,1024]{1,0:T(8,128)(2,1)S(1)}, u32[]{:S(2)}, u32[]{:S(2)}) collective-permute-start(bf16[32,1024]{1,0:T(8,128)(2,1)S(1)} %collective-permute-done.4), channel_id=1, source_target_pairs={{0,1},{1,2},{2,3},{3,4},{4,5},{5,6},{6,7},{7,8},{8,9},{9,10},{10,1... | collective-permute-start | bytes 196616 | tf_op jit(solution)/shard_map/ppermute | solution.py:24
  41.9 6.4 %collective-permute-start.12 = (bf16[32,1024]{1,0:T(8,128)(2,1)S(1)}, bf16[32,1024]{1,0:T(8,128)(2,1)S(1)}, u32[]{:S(2)}, u32[]{:S(2)}) collective-permute-start(bf16[32,1024]{1,0:T(8,128)(2,1)S(1)} %collective-permute-done.11), channel_id=1, source_target_pairs={{1,0},{2,1},{3,2},{4,3},{5,4},{6,5},{7,6},{8,7},{9,8},{10,9},{11,1... | collective-permute-start | bytes 196616 | tf_op jit(solution)/shard_map/ppermute | solution.py:26
  47.0 7.2 %collective-permute-start.6 = (bf16[32,1024]{1,0:T(8,128)(2,1)S(1)}, bf16[32,1024]{1,0:T(8,128)(2,1)S(1)}, u32[]{:S(2)}, u32[]{:S(2)}) collective-permute-start(bf16[32,1024]{1,0:T(8,128)(2,1)S(1)} %collective-permute-done.5), channel_id=1, source_target_pairs={{0,1},{1,2},{2,3},{3,4},{4,5},{5,6},{6,7},{7,8},{8,9},{9,10},{10,1... | collective-permute-start | bytes 196616 | tf_op jit(solution)/shard_map/ppermute | solution.py:24
  48.3 7.3 %collective-permute-start.13 = (bf16[32,1024]{1,0:T(8,128)(2,1)S(1)}, bf16[32,1024]{1,0:T(8,128)(2,1)S(1)}, u32[]{:S(2)}, u32[]{:S(2)}) collective-permute-start(bf16[32,1024]{1,0:T(8,128)(2,1)S(1)} %collective-permute-done.12), channel_id=1, source_target_pairs={{1,0},{2,1},{3,2},{4,3},{5,4},{6,5},{7,6},{8,7},{9,8},{10,9},{11,1... | collective-permute-start | bytes 196616 | tf_op jit(solution)/shard_map/ppermute | solution.py:26
  54.2 6.4 %collective-permute-start.7 = (bf16[32,1024]{1,0:T(8,128)(2,1)S(1)}, bf16[32,1024]{1,0:T(8,128)(2,1)S(1)}, u32[]{:S(2)}, u32[]{:S(2)}) collective-permute-start(bf16[32,1024]{1,0:T(8,128)(2,1)S(1)} %collective-permute-done.6), channel_id=1, source_target_pairs={{0,1},{1,2},{2,3},{3,4},{4,5},{5,6},{6,7},{7,8},{8,9},{9,10},{10,1... | collective-permute-start | bytes 196616 | tf_op jit(solution)/shard_map/ppermute | solution.py:24
  55.5 7.6 %collective-permute-start.14 = (bf16[32,1024]{1,0:T(8,128)(2,1)S(1)}, bf16[32,1024]{1,0:T(8,128)(2,1)S(1)}, u32[]{:S(2)}, u32[]{:S(2)}) collective-permute-start(bf16[32,1024]{1,0:T(8,128)(2,1)S(1)} %collective-permute-done.13), channel_id=1, source_target_pairs={{1,0},{2,1},{3,2},{4,3},{5,4},{6,5},{7,6},{8,7},{9,8},{10,9},{11,1... | collective-permute-start | bytes 196616 | tf_op jit(solution)/shard_map/ppermute | solution.py:26
  77.7 2.9 %copy-start.1 = (bf16[1024,1024]{1,0:T(8,128)(2,1)S(1)}, bf16[1024,1024]{1,0:T(8,128)(2,1)}, u32[]{:S(2)}) copy-start(bf16[1024,1024]{1,0:T(8,128)(2,1)} %all-gather.2.cloned.1.call-done) | copy-start | bytes 6291460
  80.6 4.2 %copy-start.2 = (f32[128,1024]{0,1:T(8,128)}, f32[128,1024]{0,1:T(8,128)S(1)}, u32[]{:S(2)}) copy-start(f32[128,1024]{0,1:T(8,128)S(1)} %get-tuple-element.16) | copy-start | bytes 1572868
  80.6 1.6 copy-start.7
  82.3 1.9 copy-start.10
  84.2 2.0 copy-start.4
  94.0 1.0 copy-start.3
  94.0 1.1 copy-start.5
  94.1 136.8 %reduce-scatter.5.cloned.1.call-start = ((), (), s32[]{:S(2)}) async-start(), calls=%async_computation.3 | async-start | bytes 4456448 | tf_op jit(solution)/shard_map/reduce_scatter | solution.py:103
  98.7 0.9 copy-start.8
  98.7 34.6 %copy-start.9 = (f32[1024]{0:T(1024)S(1)}, f32[1024]{0:T(1024)}, u32[]{:S(2)}) copy-start(f32[1024]{0:T(1024)} %param.19) | copy-start | bytes 12292
  99.6 132.3 %copy-start.6 = (f32[64,1024]{1,0:T(8,128)S(1)}, f32[64,1024]{1,0:T(8,128)}, u32[]{:S(2)}) copy-start(f32[64,1024]{1,0:T(8,128)} %param.18) | copy-start | bytes 786436
Sparse Core Ops, SparseCore 0:
  34.3 43.4 all-gather.1
  94.2 60.7 reduce-scatter.6
  159.4 71.3 reduce-scatter.4
